TPU v7x, 32 devices: a whole 2x2x4 slice. The times are simulated.
32 devices in a mesh: section: 4 (over y, x), expert: 8 (over z, core).
Axes of the slice: x: 2, y: 2, z: 4, core: 2. Of those that a mesh axis runs over, the one named last changes fastest.
Arguments:
- tokens: bfloat16 [4, 2, 256, 2048], P('section', None, 'expert'), may hold values from -6 to 6
- routes: int32 [4, 2, 256, 2], P('section', None, 'expert'), may hold values from 0 to 3, all different within a row; in each aligned block of 32 rows (0 to 31, 32 to 63, ..., all dimensions but the last counted through in order) at most 24 rows name the same one
- combine_weights: float32 [4, 2, 256, 2], P('section', None, 'expert'), may hold values from 0.3 to 1
- norm_gain: float32 [4, 2048], P('section'), may hold values from 0.5 to 1.5
- gate_up: bfloat16 [4, 8, 2048, 768], P('section', 'expert'), may hold values from -0.125 to 0.125
- down: bfloat16 [4, 8, 384, 2048], P('section', 'expert'), may hold values from -0.21875 to 0.21875
Outputs:
- next_inputs: bfloat16 [4, 2, 256, 2048], P('section', None, 'expert')
Inputs may be any that keep to these rules, and one draw needn't show every extreme that they name: `routes`: each token names 2 different experts. Among the 32 tokens of one device in one section and micro-batch (aligned blocks of 32 rows) no expert is named more than 24 times.
All inputs are finite; a program needn't handle non-finite values.
Results may differ from a plain program's by a relative error of at most 0.0055.
Values may be sent and summed in bfloat16 or wider, within the bound.
No kernel may reach another device: no remote copies, remote signals or barrier semaphores. Data moves between devices by JAX's collectives and lax.ppermute only.
A program may use at most 64 MiB of HBM per device.

v0:
```python
import jax
import jax.numpy as jnp
from jax import lax
from jax.experimental import pallas as pl
from jax.sharding import Mesh
from jax.sharding import PartitionSpec as P

EPSILON = 1e-06


def from_behind(value, axis, steps):
    count = lax.axis_size(axis)
    pairs = [(source, (source + steps) % count) for source in range(count)]
    return lax.ppermute(value, axis, pairs)


def swap_cores(value):
    return lax.ppermute(value, "core", [(0, 1), (1, 0)])


def expert_up(token_rows, weights_gu, units):
    joined = jnp.dot(token_rows, weights_gu, preferred_element_type=jnp.float32)
    return (jax.nn.silu(joined[:, :units]) * joined[:, units:]).astype(jnp.bfloat16)


def expert_down(hidden, weights_dn):
    partial_out = jnp.dot(hidden, weights_dn, preferred_element_type=jnp.float32)
    return partial_out.astype(jnp.bfloat16)


def prepare_kernel(x_ref, gain_ref, route_ref, weight_ref, buffer_ref, mixing_ref, *, experts, capacity):
    micro, topk, tok_count = route_ref.shape
    width = x_ref.shape[-1]
    block = micro * capacity
    slots = experts * block
    values = x_ref[...].astype(jnp.float32)
    scale = lax.rsqrt(jnp.mean(values * values, axis=-1, keepdims=True) + EPSILON)
    normed = (values * scale * gain_ref[...]).astype(jnp.bfloat16)
    upper = (
        lax.broadcasted_iota(jnp.int32, (tok_count, tok_count), 0)
        < lax.broadcasted_iota(jnp.int32, (tok_count, tok_count), 1)
    ).astype(jnp.float32)
    names = lax.broadcasted_iota(jnp.int32, (experts, tok_count), 0)
    lanes = lax.broadcasted_iota(jnp.int32, (slots, tok_count), 0)
    buffer = jnp.zeros((slots, width), jnp.float32)
    for m in range(micro):
        routes = route_ref[m]
        weights = weight_ref[m]
        offset = jnp.zeros((experts, 1), jnp.float32)
        hit = jnp.zeros((slots, tok_count), jnp.float32)
        mixing = jnp.zeros((slots, tok_count), jnp.float32)
        for k in range(topk):
            chosen = routes[k : k + 1, :]
            pick = (chosen == names).astype(jnp.float32)
            before = jnp.dot(pick, upper, preferred_element_type=jnp.float32) + offset
            slot = jnp.sum(before * pick, axis=0, keepdims=True).astype(jnp.int32)
            place = chosen * block + m * capacity + slot
            match = place == lanes
            hit = jnp.maximum(hit, match.astype(jnp.float32))
            mixing = mixing + jnp.where(match, weights[k : k + 1, :], 0.0)
            offset = offset + jnp.sum(pick, axis=1, keepdims=True)
        rows = normed[m * tok_count : (m + 1) * tok_count, :]
        buffer = buffer + jnp.dot(hit.astype(jnp.bfloat16), rows, preferred_element_type=jnp.float32)
        mixing_ref[m] = mixing
    buffer_ref[...] = buffer.astype(jnp.bfloat16)


def prepare(inputs, gain, routes, weights, experts, capacity):
    micro, tok_count, width = inputs.shape
    slots = experts * micro * capacity
    return pl.pallas_call(
        lambda *refs: prepare_kernel(*refs, experts=experts, capacity=capacity),
        out_shape=(
            jax.ShapeDtypeStruct((slots, width), jnp.bfloat16),
            jax.ShapeDtypeStruct((micro, slots, tok_count), jnp.float32),
        ),
    )(
        inputs.reshape(micro * tok_count, width),
        gain.reshape(1, width),
        jnp.swapaxes(routes, 1, 2),
        jnp.swapaxes(weights, 1, 2),
    )


def body(tokens, routes, combine_weights, norm_gain, gate_up, down):
    inputs = tokens[0]
    micro, tok_count, width = inputs.shape
    experts = lax.axis_size("z")
    topk = routes.shape[3]
    capacity = 2 * ((3 * tok_count * topk + 4 * experts - 1) // (4 * experts))
    block = micro * capacity
    buffer, mixing = prepare(inputs, norm_gain[0], routes[0], combine_weights[0], experts, capacity)
    buffer = buffer.reshape(experts, block, width)
    incoming = lax.all_to_all(buffer, "z", split_axis=0, concat_axis=0, tiled=True)
    units = down.shape[2]
    partner_rows = swap_cores(incoming)
    own_hidden = expert_up(incoming.reshape(-1, width), gate_up[0, 0], units)
    lent_hidden = expert_up(partner_rows.reshape(-1, width), gate_up[0, 0], units)
    lent = expert_down(lent_hidden, down[0, 0])
    other_half = swap_cores(lent.reshape(incoming.shape))
    own = expert_down(own_hidden, down[0, 0])
    results = (own.reshape(incoming.shape).astype(jnp.float32) + other_half.astype(jnp.float32))
    results = results.astype(jnp.bfloat16)
    returned = lax.all_to_all(results, "z", split_axis=0, concat_axis=0, tiled=True)
    table = returned.reshape(-1, width)
    combined = jnp.einsum(
        "mqt,qd->mtd",
        mixing,
        table.astype(jnp.float32),
        precision=lax.Precision.HIGHEST,
        preferred_element_type=jnp.float32,
    )
    mixed = inputs.astype(jnp.float32) + combined
    moved = from_behind(mixed.astype(jnp.bfloat16), "section", 1)
    return moved[None]


def solution(mesh):
    sections, spread = mesh.devices.shape
    chips = Mesh(mesh.devices.reshape(sections, spread // 2, 2), ("section", "z", "core"))
    split = ("z", "core")
    return jax.shard_map(
        body,
        mesh=chips,
        in_specs=(
            P("section", None, split, None),
            P("section", None, split, None),
            P("section", None, split, None),
            P("section", None),
            P("section", split, None, None),
            P("section", split, None, None),
        ),
        out_specs=P("section", None, split, None),
        check_vma=False,
    )
```

profile of v0, /device:TPU:0, one launch (start us, length us, event | category | flops | bytes accessed | tf_op | source)
XLA Modules:
  0.0 68.9 jit_solution(17161683371385563528)
XLA Ops:
  0.0 0.0 copy-start
  0.0 2.7 %shard_map.64 = (bf16[192,2048]{1,0:T(8,128)(2,1)}, f32[2,192,32]{2,1,0:T(8,128)}) custom-call(bf16[64,2048]{1,0:T(8,128)(2,1)} %bitcast.36, f32[1,2048]{1,0:T(1,128)} %refs_1_.1, s32[2,2,32]{2,1,0:T(2,128)} %bitcast.41, f32[2,2,32]{2,1,0:T(2,128)} %bitcast.42), custom_call_target="tpu_custom_call" | custom-call | tf_op jit(solution)/shard_map/pallas_call | solution.py:71
  2.7 26.5 %all_to_all.10 = bf16[4,48,2048]{2,1,0:T(8,128)(2,1)S(1)} all-to-all(bf16[4,48,2048]{2,1,0:T(8,128)(2,1)} %bitcast.37), channel_id=1, replica_groups=mesh['section'=4,'z'=4,'core'=2] {'z'}, dimensions={0} | all-to-all | bytes 1572864 | tf_op jit(solution)/shard_map/all_to_all | solution.py:94
  29.2 0.0 collective-permute-start
  29.2 2.3 %collective-permute-done = bf16[4,48,2048]{2,1,0:T(8,128)(2,1)S(1)} collective-permute-done((bf16[4,48,2048]{2,1,0:T(8,128)(2,1)S(1)}, bf16[4,48,2048]{2,1,0:T(8,128)(2,1)S(1)}, u32[]{:S(2)}, u32[]{:S(2)}) %collective-permute-start) | collective-permute-done | bytes 786464 | tf_op jit(solution)/shard_map/ppermute | solution.py:18
  31.5 0.0 copy-done
  31.5 0.0 copy-start.3
  31.5 0.8 %fusion = f32[192,768]{1,0:T(8,128)S(1)} fusion(bf16[192,2048]{1,0:T(8,128)(2,1)S(1)} %bitcast.39, bf16[1,1,2048,768]{3,2,1,0:T(8,128)(2,1)S(1)} %copy-done), kind=kOutput, calls=%fused_computation | convolution fusion | flops 603979776 | bytes 4521984 | tf_op jit(solution)/shard_map/dot_general | solution.py:22
  32.3 0.6 copy-done.3
  32.9 0.6 convolution_convert_fusion
  33.5 0.2 collective-permute-start.1
  33.7 0.8 %fusion.2 = f32[192,768]{1,0:T(8,128)S(1)} fusion(bf16[192,2048]{1,0:T(8,128)(2,1)S(1)} %bitcast.35, bf16[1,1,2048,768]{3,2,1,0:T(8,128)(2,1)S(1)} %copy-done), kind=kOutput, calls=%fused_computation.2 | convolution fusion | flops 603979776 | bytes 4521984 | tf_op jit(solution)/shard_map/dot_general | solution.py:22
  34.5 0.6 convolution_convert_fusion.1
  35.1 0.8 %collective-permute-done.1 = bf16[4,48,2048]{2,1,0:T(8,128)(2,1)S(1)} collective-permute-done((bf16[4,48,2048]{2,1,0:T(8,128)(2,1)S(1)}, bf16[4,48,2048]{2,1,0:T(8,128)(2,1)S(1)}, u32[]{:S(2)}, u32[]{:S(2)}) %collective-permute-start.1) | collective-permute-done | bytes 786464 | tf_op jit(solution)/shard_map/ppermute | solution.py:18
  35.8 0.0 copy-start.1
  35.8 0.0 copy-start.2
  35.8 0.3 fusion.5
  36.1 23.1 %all_to_all.11 = bf16[4,48,2048]{2,1,0:T(8,128)(2,1)S(1)} all-to-all(bf16[4,48,2048]{2,1,0:T(8,128)(2,1)S(1)} %fusion.5), channel_id=1, replica_groups=mesh['section'=4,'z'=4,'core'=2] {'z'}, dimensions={0} | all-to-all | bytes 1572864 | tf_op jit(solution)/shard_map/all_to_all | solution.py:104
  59.2 0.0 copy-done.1
  59.2 0.0 copy-done.2
  59.2 0.6 fusion.4
  59.8 1.5 %collective-permute-start.2 = (bf16[2,32,2048]{2,1,0:T(8,128)(2,1)S(1)}, bf16[2,32,2048]{2,1,0:T(8,128)(2,1)S(1)}, u32[]{:S(2)}, u32[]{:S(2)}) collective-permute-start(bf16[2,32,2048]{2,1,0:T(8,128)(2,1)S(1)} %fusion.4), channel_id=1, source_target_pairs={{0,8},{8,16},{16,24},{24,0},{1,9},{9,17},{17,25},{25,1},{2,10},{10... | collective-permute-start | bytes 786440 | tf_op jit(solution)/shard_map/ppermute | solution.py:14
  61.4 6.8 %collective-permute-done.2 = bf16[2,32,2048]{2,1,0:T(8,128)(2,1)S(1)} collective-permute-done((bf16[2,32,2048]{2,1,0:T(8,128)(2,1)S(1)}, bf16[2,32,2048]{2,1,0:T(8,128)(2,1)S(1)}, u32[]{:S(2)}, u32[]{:S(2)}) %collective-permute-start.2) | collective-permute-done | bytes 262176 | tf_op jit(solution)/shard_map/ppermute | solution.py:14
  68.2 0.7 %copy.10 = bf16[1,2,32,2048]{3,2,1,0:T(8,128)(2,1)} copy(bf16[1,2,32,2048]{3,2,1,0:T(8,128)(2,1)S(1)} %bitcast.40) | data formatting | bytes 524288
Async XLA Ops:
  0.0 31.5 %copy-start = (bf16[1,1,2048,768]{3,2,1,0:T(8,128)(2,1)S(1)}, bf16[1,1,2048,768]{3,2,1,0:T(8,128)(2,1)}, u32[]{:S(2)}) copy-start(bf16[1,1,2048,768]{3,2,1,0:T(8,128)(2,1)} %param.10) | copy-start | bytes 9437188
  29.2 2.3 %collective-permute-start = (bf16[4,48,2048]{2,1,0:T(8,128)(2,1)S(1)}, bf16[4,48,2048]{2,1,0:T(8,128)(2,1)S(1)}, u32[]{:S(2)}, u32[]{:S(2)}) collective-permute-start(bf16[4,48,2048]{2,1,0:T(8,128)(2,1)S(1)} %all_to_all.10), channel_id=1, source_target_pairs={{0,1},{1,0},{2,3},{3,2},{4,5},{5,4},{6,7},{7,6},{8,9},{9,8},{10,11... | collective-permute-start | bytes 2359304 | tf_op jit(solution)/shard_map/ppermute | solution.py:18
  31.5 1.4 %copy-start.3 = (bf16[1,1,384,2048]{3,2,1,0:T(8,128)(2,1)S(1)}, bf16[1,1,384,2048]{3,2,1,0:T(8,128)(2,1)}, u32[]{:S(2)}) copy-start(bf16[1,1,384,2048]{3,2,1,0:T(8,128)(2,1)} %param.11) | copy-start | bytes 4718596
  33.5 2.4 %collective-permute-start.1 = (bf16[4,48,2048]{2,1,0:T(8,128)(2,1)S(1)}, bf16[4,48,2048]{2,1,0:T(8,128)(2,1)S(1)}, u32[]{:S(2)}, u32[]{:S(2)}) collective-permute-start(bf16[4,48,2048]{2,1,0:T(8,128)(2,1)S(1)} %bitcast.43), channel_id=1, source_target_pairs={{0,1},{1,0},{2,3},{3,2},{4,5},{5,4},{6,7},{7,6},{8,9},{9,8},{10,11... | collective-permute-start | bytes 2359304 | tf_op jit(solution)/shard_map/ppermute | solution.py:18
  35.8 23.4 %copy-start.1 = (bf16[1,2,32,2048]{3,2,1,0:T(8,128)(2,1)S(1)}, bf16[1,2,32,2048]{3,2,1,0:T(8,128)(2,1)}, u32[]{:S(2)}) copy-start(bf16[1,2,32,2048]{3,2,1,0:T(8,128)(2,1)} %param.6) | copy-start | bytes 786436
  35.8 23.4 %copy-start.2 = (f32[2,192,32]{2,1,0:T(8,128)S(1)}, f32[2,192,32]{2,1,0:T(8,128)}, u32[]{:S(2)}) copy-start(f32[2,192,32]{2,1,0:T(8,128)} %get-tuple-element.7) | copy-start | bytes 147460
  59.8 8.3 %collective-permute-start.2 = (bf16[2,32,2048]{2,1,0:T(8,128)(2,1)S(1)}, bf16[2,32,2048]{2,1,0:T(8,128)(2,1)S(1)}, u32[]{:S(2)}, u32[]{:S(2)}) collective-permute-start(bf16[2,32,2048]{2,1,0:T(8,128)(2,1)S(1)} %fusion.4), channel_id=1, source_target_pairs={{0,8},{8,16},{16,24},{24,0},{1,9},{9,17},{17,25},{25,1},{2,10},{10... | collective-permute-start | bytes 786440 | tf_op jit(solution)/shard_map/ppermute | solution.py:14
where the time goes:
time: 69.1 us; the launch traced here: 68.9 us
  blocking collectives  49.6 us (72%)
  waiting for transfers between devices  9.82 us (14%)
  matrix products  3.35 us (5%)
  Pallas kernels  2.71 us (4%)
  starting transfers between devices  1.75 us (3%)
  local copies, waits for them, and re-layouts  1.34 us (2%)
    all_to_all x1, blocking collectives, body(): lax.all_to_all(buffer, 'z', split_axis=0, concat_axis=0, tiled=True)  26.5 us
    all_to_all x1, blocking collectives, body(): lax.all_to_all(results, 'z', split_axis=0, concat_axis=0, tiled=True)  23.1 us
    ppermute x1, waiting for transfers between devices, from_behind(): return lax.ppermute(value, axis, pairs)  6.78 us
    ppermute x2, waiting for transfers between devices, swap_cores(): return lax.ppermute(value, 'core', [(0, 1), (1, 0)])  3.04 us
    pallas_call x1, Pallas kernels, prepare(): pl.pallas_call(lambda *refs: prepare_kernel(*refs, experts=experts, capac...  2.71 us
    dot_general x2, matrix products, expert_up(): joined = jnp.dot(token_rows, weights_gu, preferred_element_type=jnp.float32)  1.55 us
    ppermute x1, starting transfers between devices, from_behind(): return lax.ppermute(value, axis, pairs)  1.54 us
  transfers between devices with their start and end apart: 3, of which 3 were waited for; matrix products, arithmetic and copies ran while one was open for 2% of the time, Pallas kernels for 0%

commit v1 on v0

--- a/solution.py
+++ b/solution.py
@@ -18,12 +18,10 @@
     return lax.ppermute(value, "core", [(0, 1), (1, 0)])
 
 
-def expert_up(token_rows, weights_gu, units):
+def expert_half(token_rows, weights_gu, weights_dn):
+    units = weights_dn.shape[0]
     joined = jnp.dot(token_rows, weights_gu, preferred_element_type=jnp.float32)
-    return (jax.nn.silu(joined[:, :units]) * joined[:, units:]).astype(jnp.bfloat16)
-
-
-def expert_down(hidden, weights_dn):
+    hidden = (jax.nn.silu(joined[:, :units]) * joined[:, units:]).astype(jnp.bfloat16)
     partial_out = jnp.dot(hidden, weights_dn, preferred_element_type=jnp.float32)
     return partial_out.astype(jnp.bfloat16)
 
@@ -92,27 +90,27 @@
     buffer, mixing = prepare(inputs, norm_gain[0], routes[0], combine_weights[0], experts, capacity)
     buffer = buffer.reshape(experts, block, width)
     incoming = lax.all_to_all(buffer, "z", split_axis=0, concat_axis=0, tiled=True)
-    units = down.shape[2]
     partner_rows = swap_cores(incoming)
-    own_hidden = expert_up(incoming.reshape(-1, width), gate_up[0, 0], units)
-    lent_hidden = expert_up(partner_rows.reshape(-1, width), gate_up[0, 0], units)
-    lent = expert_down(lent_hidden, down[0, 0])
+    own = expert_half(incoming.reshape(-1, width), gate_up[0, 0], down[0, 0])
+    lent = expert_half(partner_rows.reshape(-1, width), gate_up[0, 0], down[0, 0])
     other_half = swap_cores(lent.reshape(incoming.shape))
-    own = expert_down(own_hidden, down[0, 0])
     results = (own.reshape(incoming.shape).astype(jnp.float32) + other_half.astype(jnp.float32))
     results = results.astype(jnp.bfloat16)
-    returned = lax.all_to_all(results, "z", split_axis=0, concat_axis=0, tiled=True)
-    table = returned.reshape(-1, width)
-    combined = jnp.einsum(
-        "mqt,qd->mtd",
-        mixing,
-        table.astype(jnp.float32),
-        precision=lax.Precision.HIGHEST,
-        preferred_element_type=jnp.float32,
-    )
-    mixed = inputs.astype(jnp.float32) + combined
-    moved = from_behind(mixed.astype(jnp.bfloat16), "section", 1)
-    return moved[None]
+    half = width // 2
+    moved = []
+    for lo, hi in ((0, half), (half, width)):
+        returned = lax.all_to_all(results[..., lo:hi], "z", split_axis=0, concat_axis=0, tiled=True)
+        table = returned.reshape(-1, hi - lo)
+        combined = jnp.einsum(
+            "mqt,qd->mtd",
+            mixing,
+            table.astype(jnp.float32),
+            precision=lax.Precision.HIGHEST,
+            preferred_element_type=jnp.float32,
+        )
+        mixed = inputs[..., lo:hi].astype(jnp.float32) + combined
+        moved.append(from_behind(mixed.astype(jnp.bfloat16), "section", 1))
+    return jnp.concatenate(moved, axis=-1)[None]
 
 
 def solution(mesh):

time: 69.1 us -> 77.8 us (1.13)
  blocking collectives: 49.6 us -> 41.8 us
  waiting for transfers between devices: 9.82 us -> 17.5 us
  starting transfers between devices: 1.75 us -> 6.7 us
  matrix products: 3.35 us -> 6.26 us
    all_to_all x0 -> x1, waiting for transfers between devices: none -> 9.23 us  [body(): lax.all_to_all(results[..., lo:hi], 'z', split_axis=0, concat_axis=0, til...]
    all_to_all x1, blocking collectives: 23.1 us -> 15.3 us  [body(): lax.all_to_all(results[..., lo:hi], 'z', split_axis=0, concat_axis=0, til...]
    all_to_all x0 -> x1, starting transfers between devices: none -> 3.46 us  [body(): lax.all_to_all(results[..., lo:hi], 'z', split_axis=0, concat_axis=0, til...]
    dot_general x1 -> x2, matrix products: 0.61 us -> 3.52 us  [body(): jnp.einsum('mqt,qd->mtd', mixing, table.astype(jnp.float32), precision=la...]
    ppermute x1 -> x2, waiting for transfers between devices: 6.78 us -> 5.26 us  [from_behind(): return lax.ppermute(value, axis, pairs)]
    ppermute x1 -> x2, starting transfers between devices: 1.54 us -> 3.03 us  [from_behind(): return lax.ppermute(value, axis, pairs)]
    slice x0 -> x1, local copies, waits for them, and re-layouts: none -> 0.8 us  [body(): results[..., lo:hi]]
  transfers between devices with their start and end apart: 3 -> 5, of which waited for: 3 -> 5; matrix products, arithmetic and copies ran while one was open for 2% -> 5% of each run, Pallas kernels for 0% -> 0%
where the time goes in v1:
time: 77.8 us; the launch traced here: 77.5 us
  blocking collectives  41.8 us (54%)
  waiting for transfers between devices  17.5 us (22%)
  starting transfers between devices  6.7 us (9%)
  matrix products  6.26 us (8%)
  Pallas kernels  2.71 us (3%)
  local copies, waits for them, and re-layouts  1.43 us (2%)
  other arithmetic  0.98 us (1%)
    all_to_all x1, blocking collectives, body(): lax.all_to_all(buffer, 'z', split_axis=0, concat_axis=0, tiled=True)  26.5 us
    all_to_all x1, blocking collectives, body(): lax.all_to_all(results[..., lo:hi], 'z', split_axis=0, concat_axis=0, til...  15.3 us
    all_to_all x1, waiting for transfers between devices, body(): lax.all_to_all(results[..., lo:hi], 'z', split_axis=0, concat_axis=0, til...  9.23 us
    ppermute x2, waiting for transfers between devices, from_behind(): return lax.ppermute(value, axis, pairs)  5.26 us
    dot_general x2, matrix products, body(): jnp.einsum('mqt,qd->mtd', mixing, table.astype(jnp.float32), precision=la...  3.52 us
    all_to_all x1, starting transfers between devices, body(): lax.all_to_all(results[..., lo:hi], 'z', split_axis=0, concat_axis=0, til...  3.46 us
    ppermute x2, waiting for transfers between devices, swap_cores(): return lax.ppermute(value, 'core', [(0, 1), (1, 0)])  3.04 us
    ppermute x2, starting transfers between devices, from_behind(): return lax.ppermute(value, axis, pairs)  3.03 us
  transfers between devices with their start and end apart: 5, of which 5 were waited for; matrix products, arithmetic and copies ran while one was open for 5% of the time, Pallas kernels for 0%

profile of v1, /device:TPU:0, one launch (start us, length us, event | category | flops | bytes accessed | tf_op | source)
XLA Modules:
  0.0 77.5 jit_solution(17924887930256272499)
XLA Ops:
  0.0 0.0 copy-start
  0.0 2.7 %shard_map.64 = (bf16[192,2048]{1,0:T(8,128)(2,1)}, f32[2,192,32]{2,1,0:T(8,128)}) custom-call(bf16[64,2048]{1,0:T(8,128)(2,1)} %bitcast.41, f32[1,2048]{1,0:T(1,128)} %refs_1_.1, s32[2,2,32]{2,1,0:T(2,128)} %bitcast.47, f32[2,2,32]{2,1,0:T(2,128)} %bitcast.48), custom_call_target="tpu_custom_call" | custom-call | tf_op jit(solution)/shard_map/pallas_call | solution.py:69
  2.7 26.5 %all_to_all.15 = bf16[4,48,2048]{2,1,0:T(8,128)(2,1)S(1)} all-to-all(bf16[4,48,2048]{2,1,0:T(8,128)(2,1)} %bitcast.44), channel_id=1, replica_groups=mesh['section'=4,'z'=4,'core'=2] {'z'}, dimensions={0} | all-to-all | bytes 1572864 | tf_op jit(solution)/shard_map/all_to_all | solution.py:92
  29.2 0.0 collective-permute-start
  29.2 2.3 %collective-permute-done = bf16[4,48,2048]{2,1,0:T(8,128)(2,1)S(1)} collective-permute-done((bf16[4,48,2048]{2,1,0:T(8,128)(2,1)S(1)}, bf16[4,48,2048]{2,1,0:T(8,128)(2,1)S(1)}, u32[]{:S(2)}, u32[]{:S(2)}) %collective-permute-start) | collective-permute-done | bytes 786464 | tf_op jit(solution)/shard_map/ppermute | solution.py:18
  31.5 0.8 %fusion = f32[192,768]{1,0:T(8,128)S(1)} fusion(bf16[192,2048]{1,0:T(8,128)(2,1)S(1)} %bitcast.46, bf16[1,1,2048,768]{3,2,1,0:T(8,128)(2,1)S(1)} %copy-done), kind=kOutput, calls=%fused_computation | convolution fusion | flops 603979776 | bytes 4521984 | tf_op jit(solution)/shard_map/dot_general | solution.py:23
  32.3 0.6 copy-done.1
  32.9 0.6 convolution_convert_fusion
  33.5 0.2 collective-permute-start.1
  33.7 0.8 %fusion.2 = f32[192,768]{1,0:T(8,128)S(1)} fusion(bf16[192,2048]{1,0:T(8,128)(2,1)S(1)} %bitcast.38, bf16[1,1,2048,768]{3,2,1,0:T(8,128)(2,1)S(1)} %copy-done), kind=kOutput, calls=%fused_computation.2 | convolution fusion | flops 603979776 | bytes 4521984 | tf_op jit(solution)/shard_map/dot_general | solution.py:23
  34.5 0.6 convolution_convert_fusion.1
  35.1 0.8 collective-permute-done.1
  35.8 0.3 fusion.4
  36.1 0.8 %fusion.17 = (bf16[4,48,1024]{2,1,0:T(8,128)(2,1)S(1)}, bf16[4,48,1024]{2,1,0:T(8,128)(2,1)}) fusion(bf16[4,48,2048]{2,1,0:T(8,128)(2,1)S(1)} %fusion.4), kind=kLoop, calls=%fused_computation.23 | loop fusion | bytes 1572864 | tf_op jit(solution)/shard_map/slice | solution.py:102
  36.9 15.3 %all_to_all.16 = bf16[4,48,1024]{2,1,0:T(8,128)(2,1)} all-to-all(bf16[4,48,1024]{2,1,0:T(8,128)(2,1)S(1)} %get-tuple-element.9), channel_id=1, replica_groups=mesh['section'=4,'z'=4,'core'=2] {'z'}, dimensions={0} | all-to-all | bytes 786432 | tf_op jit(solution)/shard_map/all_to_all | solution.py:102
  52.2 3.5 %all-to-all-start.2 = ((bf16[4,48,1024]{2,1,0:T(8,128)(2,1)}), bf16[4,48,1024]{2,1,0:T(8,128)(2,1)S(1)}, u32[]{:S(2)}, u32[]{:S(2)}) async-start(bf16[4,48,1024]{2,1,0:T(8,128)(2,1)} %get-tuple-element.10), calls=%async_computation.2 | async-start | bytes 786432 | tf_op jit(solution)/shard_map/all_to_all | solution.py:102
  55.7 2.1 %fusion.7 = bf16[2,32,1024]{2,1,0:T(8,128)(2,1)} fusion(f32[2,192,32]{2,1,0:T(8,128)} %get-tuple-element.7, bf16[192,1024,1]{1,0,2:T(8,128)(2,1)} %bitcast.40, bf16[2,32,2048]{2,1,0:T(8,128)(2,1)} %bitcast.42), kind=kOutput, calls=%fused_computation.12 | convolution fusion | flops 151191552 | bytes 704512 | tf_op jit(solution)/shard_map/mqt,qd->mtd/dot_general | solution.py:104
  57.8 9.2 %all-to-all-done.2 = bf16[4,48,1024]{2,1,0:T(8,128)(2,1)S(1)} async-done(((bf16[4,48,1024]{2,1,0:T(8,128)(2,1)}), bf16[4,48,1024]{2,1,0:T(8,128)(2,1)S(1)}, u32[]{:S(2)}, u32[]{:S(2)}) %all-to-all-start.2) | async-done | bytes 393248 | tf_op jit(solution)/shard_map/all_to_all | solution.py:102
  67.1 1.4 %fusion.8 = bf16[2,32,1024]{2,1,0:T(8,128)(2,1)S(1)} fusion(f32[2,192,32]{2,1,0:T(8,128)} %get-tuple-element.7, bf16[192,1024,1]{1,0,2:T(8,128)(2,1)S(1)} %bitcast.39, bf16[2,32,2048]{2,1,0:T(8,128)(2,1)} %bitcast.43), kind=kOutput, calls=%fused_computation.13 | convolution fusion | flops 151191552 | bytes 704512 | tf_op jit(solution)/shard_map/mqt,qd->mtd/dot_general | solution.py:104
  68.4 1.5 %collective-permute-start.3 = (bf16[2,32,1024]{2,1,0:T(8,128)(2,1)S(1)}, bf16[2,32,1024]{2,1,0:T(8,128)(2,1)S(1)}, u32[]{:S(2)}, u32[]{:S(2)}) collective-permute-start(bf16[2,32,1024]{2,1,0:T(8,128)(2,1)S(1)} %fusion.8), channel_id=1, source_target_pairs={{0,8},{8,16},{16,24},{24,0},{1,9},{9,17},{17,25},{25,1},{2,10},{10... | collective-permute-start | bytes 393224 | tf_op jit(solution)/shard_map/ppermute | solution.py:14
  70.0 1.5 %collective-permute-start.2 = (bf16[2,32,1024]{2,1,0:T(8,128)(2,1)}, bf16[2,32,1024]{2,1,0:T(8,128)(2,1)S(1)}, u32[]{:S(2)}, u32[]{:S(2)}) collective-permute-start(bf16[2,32,1024]{2,1,0:T(8,128)(2,1)} %fusion.7), channel_id=1, source_target_pairs={{0,8},{8,16},{16,24},{24,0},{1,9},{9,17},{17,25},{25,1},{2,10},{10... | collective-permute-start | bytes 393224 | tf_op jit(solution)/shard_map/ppermute | solution.py:14
  71.5 3.9 %collective-permute-done.3 = bf16[2,32,1024]{2,1,0:T(8,128)(2,1)S(1)} collective-permute-done((bf16[2,32,1024]{2,1,0:T(8,128)(2,1)S(1)}, bf16[2,32,1024]{2,1,0:T(8,128)(2,1)S(1)}, u32[]{:S(2)}, u32[]{:S(2)}) %collective-permute-start.3) | collective-permute-done | bytes 131104 | tf_op jit(solution)/shard_map/ppermute | solution.py:14
  75.3 1.4 %collective-permute-done.2 = bf16[2,32,1024]{2,1,0:T(8,128)(2,1)S(1)} collective-permute-done((bf16[2,32,1024]{2,1,0:T(8,128)(2,1)}, bf16[2,32,1024]{2,1,0:T(8,128)(2,1)S(1)}, u32[]{:S(2)}, u32[]{:S(2)}) %collective-permute-start.2) | collective-permute-done | bytes 131104 | tf_op jit(solution)/shard_map/ppermute | solution.py:14
  76.7 0.7 maximum_bitcast_fusion
  (2 shorter events, 0.0 us)
Async XLA Ops:
  0.0 31.5 %copy-start = (bf16[1,1,2048,768]{3,2,1,0:T(8,128)(2,1)S(1)}, bf16[1,1,2048,768]{3,2,1,0:T(8,128)(2,1)}, u32[]{:S(2)}) copy-start(bf16[1,1,2048,768]{3,2,1,0:T(8,128)(2,1)} %param.10) | copy-start | bytes 9437188
  29.2 2.3 %collective-permute-start = (bf16[4,48,2048]{2,1,0:T(8,128)(2,1)S(1)}, bf16[4,48,2048]{2,1,0:T(8,128)(2,1)S(1)}, u32[]{:S(2)}, u32[]{:S(2)}) collective-permute-start(bf16[4,48,2048]{2,1,0:T(8,128)(2,1)S(1)} %all_to_all.15), channel_id=1, source_target_pairs={{0,1},{1,0},{2,3},{3,2},{4,5},{5,4},{6,7},{7,6},{8,9},{9,8},{10,11... | collective-permute-start | bytes 2359304 | tf_op jit(solution)/shard_map/ppermute | solution.py:18
  31.5 1.4 %copy-start.1 = (bf16[1,1,384,2048]{3,2,1,0:T(8,128)(2,1)S(1)}, bf16[1,1,384,2048]{3,2,1,0:T(8,128)(2,1)}, u32[]{:S(2)}) copy-start(bf16[1,1,384,2048]{3,2,1,0:T(8,128)(2,1)} %param.11) | copy-start | bytes 4718596
  33.5 2.4 %collective-permute-start.1 = (bf16[4,48,2048]{2,1,0:T(8,128)(2,1)S(1)}, bf16[4,48,2048]{2,1,0:T(8,128)(2,1)S(1)}, u32[]{:S(2)}, u32[]{:S(2)}) collective-permute-start(bf16[4,48,2048]{2,1,0:T(8,128)(2,1)S(1)} %bitcast.49), channel_id=1, source_target_pairs={{0,1},{1,0},{2,3},{3,2},{4,5},{5,4},{6,7},{7,6},{8,9},{9,8},{10,11... | collective-permute-start | bytes 2359304 | tf_op jit(solution)/shard_map/ppermute | solution.py:18
  52.2 14.8 %all-to-all-start.2 = ((bf16[4,48,1024]{2,1,0:T(8,128)(2,1)}), bf16[4,48,1024]{2,1,0:T(8,128)(2,1)S(1)}, u32[]{:S(2)}, u32[]{:S(2)}) async-start(bf16[4,48,1024]{2,1,0:T(8,128)(2,1)} %get-tuple-element.10), calls=%async_computation.2 | async-start | bytes 786432 | tf_op jit(solution)/shard_map/all_to_all | solution.py:102
  68.4 6.9 %collective-permute-start.3 = (bf16[2,32,1024]{2,1,0:T(8,128)(2,1)S(1)}, bf16[2,32,1024]{2,1,0:T(8,128)(2,1)S(1)}, u32[]{:S(2)}, u32[]{:S(2)}) collective-permute-start(bf16[2,32,1024]{2,1,0:T(8,128)(2,1)S(1)} %fusion.8), channel_id=1, source_target_pairs={{0,8},{8,16},{16,24},{24,0},{1,9},{9,17},{17,25},{25,1},{2,10},{10... | collective-permute-start | bytes 393224 | tf_op jit(solution)/shard_map/ppermute | solution.py:14
  70.0 6.7 %collective-permute-start.2 = (bf16[2,32,1024]{2,1,0:T(8,128)(2,1)}, bf16[2,32,1024]{2,1,0:T(8,128)(2,1)S(1)}, u32[]{:S(2)}, u32[]{:S(2)}) collective-permute-start(bf16[2,32,1024]{2,1,0:T(8,128)(2,1)} %fusion.7), channel_id=1, source_target_pairs={{0,8},{8,16},{16,24},{24,0},{1,9},{9,17},{17,25},{25,1},{2,10},{10... | collective-permute-start | bytes 393224 | tf_op jit(solution)/shard_map/ppermute | solution.py:14

commit v2 on v0

--- a/solution.py
+++ b/solution.py
@@ -18,12 +18,10 @@
     return lax.ppermute(value, "core", [(0, 1), (1, 0)])
 
 
-def expert_up(token_rows, weights_gu, units):
+def expert_half(token_rows, weights_gu, weights_dn):
+    units = weights_dn.shape[0]
     joined = jnp.dot(token_rows, weights_gu, preferred_element_type=jnp.float32)
-    return (jax.nn.silu(joined[:, :units]) * joined[:, units:]).astype(jnp.bfloat16)
-
-
-def expert_down(hidden, weights_dn):
+    hidden = (jax.nn.silu(joined[:, :units]) * joined[:, units:]).astype(jnp.bfloat16)
     partial_out = jnp.dot(hidden, weights_dn, preferred_element_type=jnp.float32)
     return partial_out.astype(jnp.bfloat16)
 
@@ -92,13 +90,15 @@
     buffer, mixing = prepare(inputs, norm_gain[0], routes[0], combine_weights[0], experts, capacity)
     buffer = buffer.reshape(experts, block, width)
     incoming = lax.all_to_all(buffer, "z", split_axis=0, concat_axis=0, tiled=True)
-    units = down.shape[2]
     partner_rows = swap_cores(incoming)
-    own_hidden = expert_up(incoming.reshape(-1, width), gate_up[0, 0], units)
-    lent_hidden = expert_up(partner_rows.reshape(-1, width), gate_up[0, 0], units)
-    lent = expert_down(lent_hidden, down[0, 0])
-    other_half = swap_cores(lent.reshape(incoming.shape))
-    own = expert_down(own_hidden, down[0, 0])
+    own = expert_half(incoming.reshape(-1, width), gate_up[0, 0], down[0, 0])
+    cut = experts // 2
+    returned_halves = []
+    for lo, hi in ((0, cut), (cut, experts)):
+        piece = partner_rows[lo:hi].reshape(-1, width)
+        lent = expert_half(piece, gate_up[0, 0], down[0, 0])
+        returned_halves.append(swap_cores(lent.reshape((hi - lo,) + incoming.shape[1:])))
+    other_half = jnp.concatenate(returned_halves)
     results = (own.reshape(incoming.shape).astype(jnp.float32) + other_half.astype(jnp.float32))
     results = results.astype(jnp.bfloat16)
     returned = lax.all_to_all(results, "z", split_axis=0, concat_axis=0, tiled=True)

time: 69.1 us -> 70.1 us (1.014)
  matrix products: 3.35 us -> 4.09 us
    ppermute x2 -> x3, waiting for transfers between devices: 3.04 us -> 2.29 us  [swap_cores(): return lax.ppermute(value, 'core', [(0, 1), (1, 0)])]
    dot_general x4 -> x6, matrix products: 2.74 us -> 3.48 us  [the longest x3 2.02 us: expert_half(): joined = jnp.dot(token_rows, weights_gu, preferred_element_type=jnp.float32)]
  transfers between devices with their start and end apart: 3 -> 4, of which waited for: 3 -> 2; matrix products, arithmetic and copies ran while one was open for 2% -> 3% of each run, Pallas kernels for 0% -> 0%
where the time goes in v2:
time: 70.1 us; the launch traced here: 69.9 us
  blocking collectives  49.7 us (71%)
  waiting for transfers between devices  9.23 us (13%)
  matrix products  4.09 us (6%)
  Pallas kernels  2.71 us (4%)
  starting transfers between devices  2.18 us (3%)
  local copies, waits for them, and re-layouts  1.57 us (2%)
    all_to_all x1, blocking collectives, body(): lax.all_to_all(buffer, 'z', split_axis=0, concat_axis=0, tiled=True)  26.5 us
    all_to_all x1, blocking collectives, body(): lax.all_to_all(results, 'z', split_axis=0, concat_axis=0, tiled=True)  23.3 us
    ppermute x1, waiting for transfers between devices, from_behind(): return lax.ppermute(value, axis, pairs)  6.94 us
    pallas_call x1, Pallas kernels, prepare(): pl.pallas_call(lambda *refs: prepare_kernel(*refs, experts=experts, capac...  2.71 us
    ppermute x3, waiting for transfers between devices, swap_cores(): return lax.ppermute(value, 'core', [(0, 1), (1, 0)])  2.29 us
    dot_general x3, matrix products, expert_half(): joined = jnp.dot(token_rows, weights_gu, preferred_element_type=jnp.float32)  2.02 us
    ppermute x1, starting transfers between devices, from_behind(): return lax.ppermute(value, axis, pairs)  1.54 us
    unnamed x9, local copies, waits for them, and re-layouts  1.5 us
  transfers between devices with their start and end apart: 4, of which 2 were waited for; matrix products, arithmetic and copies ran while one was open for 3% of the time, Pallas kernels for 0%

profile of v2, /device:TPU:0, one launch (start us, length us, event | category | flops | bytes accessed | tf_op | source)
XLA Modules:
  0.0 69.9 jit_solution(16359197354399758838)
XLA Ops:
  0.0 2.7 %shard_map.64 = (bf16[192,2048]{1,0:T(8,128)(2,1)}, f32[2,192,32]{2,1,0:T(8,128)}) custom-call(bf16[64,2048]{1,0:T(8,128)(2,1)} %bitcast.45, f32[1,2048]{1,0:T(1,128)} %refs_1_.1, s32[2,2,32]{2,1,0:T(2,128)} %bitcast.51, f32[2,2,32]{2,1,0:T(2,128)} %bitcast.52), custom_call_target="tpu_custom_call" | custom-call | tf_op jit(solution)/shard_map/pallas_call | solution.py:69
  2.7 26.5 %all_to_all.10 = bf16[4,48,2048]{2,1,0:T(8,128)(2,1)S(1)} all-to-all(bf16[4,48,2048]{2,1,0:T(8,128)(2,1)} %bitcast.46), channel_id=1, replica_groups=mesh['section'=4,'z'=4,'core'=2] {'z'}, dimensions={0} | all-to-all | bytes 1572864 | tf_op jit(solution)/shard_map/all_to_all | solution.py:92
  29.2 0.0 collective-permute-start
  29.2 2.3 %collective-permute-done = bf16[4,48,2048]{2,1,0:T(8,128)(2,1)S(1)} collective-permute-done((bf16[4,48,2048]{2,1,0:T(8,128)(2,1)S(1)}, bf16[4,48,2048]{2,1,0:T(8,128)(2,1)S(1)}, u32[]{:S(2)}, u32[]{:S(2)}) %collective-permute-start) | collective-permute-done | bytes 786464 | tf_op jit(solution)/shard_map/ppermute | solution.py:18
  31.5 0.1 fusion.23
  31.5 0.0 copy-start.1
  31.6 0.6 fusion.2
  32.2 0.8 %copy-done.1 = bf16[1,1,384,2048]{3,2,1,0:T(8,128)(2,1)S(1)} copy-done((bf16[1,1,384,2048]{3,2,1,0:T(8,128)(2,1)S(1)}, bf16[1,1,384,2048]{3,2,1,0:T(8,128)(2,1)}, u32[]{:S(2)}) %copy-start.1) | copy-done | bytes 1572888
  33.0 0.4 convolution_convert_fusion.2
  33.4 0.2 collective-permute-start.1
  33.6 0.6 fusion
  34.2 0.4 convolution_convert_fusion.1
  34.6 0.4 collective-permute-start.2
  35.1 0.8 %fusion.4 = f32[192,768]{1,0:T(8,128)S(1)} fusion(bf16[192,2048]{1,0:T(8,128)(2,1)S(1)} %bitcast.42, bf16[1,1,2048,768]{3,2,1,0:T(8,128)(2,1)S(1)} %copy-done), kind=kOutput, calls=%fused_computation.4 | convolution fusion | flops 603979776 | bytes 4521984 | tf_op jit(solution)/shard_map/dot_general | solution.py:23
  35.9 0.6 convolution_convert_fusion
  36.5 0.0 collective-permute-done.2
  36.5 0.0 copy-start.2
  36.5 0.0 copy-start.3
  36.5 0.3 fusion.7
  36.8 23.3 %all_to_all.11 = bf16[4,48,2048]{2,1,0:T(8,128)(2,1)S(1)} all-to-all(bf16[4,48,2048]{2,1,0:T(8,128)(2,1)S(1)} %fusion.7), channel_id=1, replica_groups=mesh['section'=4,'z'=4,'core'=2] {'z'}, dimensions={0} | all-to-all | bytes 1572864 | tf_op jit(solution)/shard_map/all_to_all | solution.py:104
  60.1 0.6 fusion.6
  60.7 1.5 %collective-permute-start.3 = (bf16[2,32,2048]{2,1,0:T(8,128)(2,1)S(1)}, bf16[2,32,2048]{2,1,0:T(8,128)(2,1)S(1)}, u32[]{:S(2)}, u32[]{:S(2)}) collective-permute-start(bf16[2,32,2048]{2,1,0:T(8,128)(2,1)S(1)} %fusion.6), channel_id=1, source_target_pairs={{0,8},{8,16},{16,24},{24,0},{1,9},{9,17},{17,25},{25,1},{2,10},{10... | collective-permute-start | bytes 786440 | tf_op jit(solution)/shard_map/ppermute | solution.py:14
  62.2 6.9 %collective-permute-done.3 = bf16[2,32,2048]{2,1,0:T(8,128)(2,1)S(1)} collective-permute-done((bf16[2,32,2048]{2,1,0:T(8,128)(2,1)S(1)}, bf16[2,32,2048]{2,1,0:T(8,128)(2,1)S(1)}, u32[]{:S(2)}, u32[]{:S(2)}) %collective-permute-start.3) | collective-permute-done | bytes 262176 | tf_op jit(solution)/shard_map/ppermute | solution.py:14
  69.2 0.7 %copy.10 = bf16[1,2,32,2048]{3,2,1,0:T(8,128)(2,1)} copy(bf16[1,2,32,2048]{3,2,1,0:T(8,128)(2,1)S(1)} %bitcast.50) | data formatting | bytes 524288
  (5 shorter events, 0.0 us)
Async XLA Ops:
  0.0 31.5 %copy-start = (bf16[1,1,2048,768]{3,2,1,0:T(8,128)(2,1)S(1)}, bf16[1,1,2048,768]{3,2,1,0:T(8,128)(2,1)}, u32[]{:S(2)}) copy-start(bf16[1,1,2048,768]{3,2,1,0:T(8,128)(2,1)} %param.10) | copy-start | bytes 9437188
  29.2 2.3 %collective-permute-start = (bf16[4,48,2048]{2,1,0:T(8,128)(2,1)S(1)}, bf16[4,48,2048]{2,1,0:T(8,128)(2,1)S(1)}, u32[]{:S(2)}, u32[]{:S(2)}) collective-permute-start(bf16[4,48,2048]{2,1,0:T(8,128)(2,1)S(1)} %all_to_all.10), channel_id=1, source_target_pairs={{0,1},{1,0},{2,3},{3,2},{4,5},{5,4},{6,7},{7,6},{8,9},{9,8},{10,11... | collective-permute-start | bytes 2359304 | tf_op jit(solution)/shard_map/ppermute | solution.py:18
  31.5 1.4 %copy-start.1 = (bf16[1,1,384,2048]{3,2,1,0:T(8,128)(2,1)S(1)}, bf16[1,1,384,2048]{3,2,1,0:T(8,128)(2,1)}, u32[]{:S(2)}) copy-start(bf16[1,1,384,2048]{3,2,1,0:T(8,128)(2,1)} %param.11) | copy-start | bytes 4718596
  33.4 3.1 %collective-permute-start.1 = (bf16[2,48,2048]{2,1,0:T(8,128)(2,1)S(1)}, bf16[2,48,2048]{2,1,0:T(8,128)(2,1)S(1)}, u32[]{:S(2)}, u32[]{:S(2)}) collective-permute-start(bf16[2,48,2048]{2,1,0:T(8,128)(2,1)S(1)} %bitcast.48), channel_id=1, source_target_pairs={{0,1},{1,0},{2,3},{3,2},{4,5},{5,4},{6,7},{7,6},{8,9},{9,8},{10,11... | collective-permute-start | bytes 1179656 | tf_op jit(solution)/shard_map/ppermute | solution.py:18
  34.6 1.8 %collective-permute-start.2 = (bf16[2,48,2048]{2,1,0:T(8,128)(2,1)S(1)}, bf16[2,48,2048]{2,1,0:T(8,128)(2,1)S(1)}, u32[]{:S(2)}, u32[]{:S(2)}) collective-permute-start(bf16[2,48,2048]{2,1,0:T(8,128)(2,1)S(1)} %bitcast.49), channel_id=1, source_target_pairs={{0,1},{1,0},{2,3},{3,2},{4,5},{5,4},{6,7},{7,6},{8,9},{9,8},{10,11... | collective-permute-start | bytes 1179656 | tf_op jit(solution)/shard_map/ppermute | solution.py:18
  36.5 23.6 %copy-start.2 = (bf16[1,2,32,2048]{3,2,1,0:T(8,128)(2,1)S(1)}, bf16[1,2,32,2048]{3,2,1,0:T(8,128)(2,1)}, u32[]{:S(2)}) copy-start(bf16[1,2,32,2048]{3,2,1,0:T(8,128)(2,1)} %param.6) | copy-start | bytes 786436
  36.5 23.5 %copy-start.3 = (f32[2,192,32]{2,1,0:T(8,128)S(1)}, f32[2,192,32]{2,1,0:T(8,128)}, u32[]{:S(2)}) copy-start(f32[2,192,32]{2,1,0:T(8,128)} %get-tuple-element.7) | copy-start | bytes 147460
  60.7 8.5 %collective-permute-start.3 = (bf16[2,32,2048]{2,1,0:T(8,128)(2,1)S(1)}, bf16[2,32,2048]{2,1,0:T(8,128)(2,1)S(1)}, u32[]{:S(2)}, u32[]{:S(2)}) collective-permute-start(bf16[2,32,2048]{2,1,0:T(8,128)(2,1)S(1)} %fusion.6), channel_id=1, source_target_pairs={{0,8},{8,16},{16,24},{24,0},{1,9},{9,17},{17,25},{25,1},{2,10},{10... | collective-permute-start | bytes 786440 | tf_op jit(solution)/shard_map/ppermute | solution.py:14

commit v3 on v2

--- a/solution.py
+++ b/solution.py
@@ -92,13 +92,8 @@
     incoming = lax.all_to_all(buffer, "z", split_axis=0, concat_axis=0, tiled=True)
     partner_rows = swap_cores(incoming)
     own = expert_half(incoming.reshape(-1, width), gate_up[0, 0], down[0, 0])
-    cut = experts // 2
-    returned_halves = []
-    for lo, hi in ((0, cut), (cut, experts)):
-        piece = partner_rows[lo:hi].reshape(-1, width)
-        lent = expert_half(piece, gate_up[0, 0], down[0, 0])
-        returned_halves.append(swap_cores(lent.reshape((hi - lo,) + incoming.shape[1:])))
-    other_half = jnp.concatenate(returned_halves)
+    lent = expert_half(partner_rows.reshape(-1, width), gate_up[0, 0], down[0, 0])
+    other_half = swap_cores(lent.reshape(incoming.shape))
     results = (own.reshape(incoming.shape).astype(jnp.float32) + other_half.astype(jnp.float32))
     results = results.astype(jnp.bfloat16)
     returned = lax.all_to_all(results, "z", split_axis=0, concat_axis=0, tiled=True)
@@ -107,7 +102,7 @@
         "mqt,qd->mtd",
         mixing,
         table.astype(jnp.float32),
-        precision=lax.Precision.HIGHEST,
+        precision=lax.Precision.HIGH,
         preferred_element_type=jnp.float32,
     )
     mixed = inputs.astype(jnp.float32) + combined

time: 70.1 us -> 68.9 us (0.983)
  matrix products: 4.09 us -> 3.19 us
    ppermute x3 -> x2, waiting for transfers between devices: 2.29 us -> 3.04 us  [swap_cores(): return lax.ppermute(value, 'core', [(0, 1), (1, 0)])]
    dot_general x3 -> x2, matrix products: 2.02 us -> 1.55 us  [expert_half(): joined = jnp.dot(token_rows, weights_gu, preferred_element_type=jnp.float32)]
    dot_general x3 -> x2, matrix products: 1.46 us -> 1.19 us  [expert_half(): jnp.dot(hidden, weights_dn, preferred_element_type=jnp.float32)]
  transfers between devices with their start and end apart: 4 -> 3, of which waited for: 2 -> 3; matrix products, arithmetic and copies ran while one was open for 3% -> 2% of each run, Pallas kernels for 0% -> 0%
where the time goes in v3:
time: 68.9 us; the launch traced here: 68.7 us
  blocking collectives  49.6 us (72%)
  waiting for transfers between devices  9.83 us (14%)
  matrix products  3.19 us (5%)
  Pallas kernels  2.71 us (4%)
  starting transfers between devices  1.75 us (3%)
  local copies, waits for them, and re-layouts  1.34 us (2%)
    all_to_all x1, blocking collectives, body(): lax.all_to_all(buffer, 'z', split_axis=0, concat_axis=0, tiled=True)  26.5 us
    all_to_all x1, blocking collectives, body(): lax.all_to_all(results, 'z', split_axis=0, concat_axis=0, tiled=True)  23.1 us
    ppermute x1, waiting for transfers between devices, from_behind(): return lax.ppermute(value, axis, pairs)  6.78 us
    ppermute x2, waiting for transfers between devices, swap_cores(): return lax.ppermute(value, 'core', [(0, 1), (1, 0)])  3.04 us
    pallas_call x1, Pallas kernels, prepare(): pl.pallas_call(lambda *refs: prepare_kernel(*refs, experts=experts, capac...  2.71 us
    dot_general x2, matrix products, expert_half(): joined = jnp.dot(token_rows, weights_gu, preferred_element_type=jnp.float32)  1.55 us
    ppermute x1, starting transfers between devices, from_behind(): return lax.ppermute(value, axis, pairs)  1.54 us
  transfers between devices with their start and end apart: 3, of which 3 were waited for; matrix products, arithmetic and copies ran while one was open for 2% of the time, Pallas kernels for 0%

profile of v3, /device:TPU:0, one launch (start us, length us, event | category | flops | bytes accessed | tf_op | source)
XLA Modules:
  0.0 68.7 jit_solution(6700490162613339565)
XLA Ops:
  0.0 0.0 copy-start
  0.0 2.7 %shard_map.64 = (bf16[192,2048]{1,0:T(8,128)(2,1)}, f32[2,192,32]{2,1,0:T(8,128)}) custom-call(bf16[64,2048]{1,0:T(8,128)(2,1)} %bitcast.36, f32[1,2048]{1,0:T(1,128)} %refs_1_.1, s32[2,2,32]{2,1,0:T(2,128)} %bitcast.41, f32[2,2,32]{2,1,0:T(2,128)} %bitcast.42), custom_call_target="tpu_custom_call" | custom-call | tf_op jit(solution)/shard_map/pallas_call | solution.py:69
  2.7 26.5 %all_to_all.10 = bf16[4,48,2048]{2,1,0:T(8,128)(2,1)S(1)} all-to-all(bf16[4,48,2048]{2,1,0:T(8,128)(2,1)} %bitcast.37), channel_id=1, replica_groups=mesh['section'=4,'z'=4,'core'=2] {'z'}, dimensions={0} | all-to-all | bytes 1572864 | tf_op jit(solution)/shard_map/all_to_all | solution.py:92
  29.2 0.0 collective-permute-start
  29.2 2.3 %collective-permute-done = bf16[4,48,2048]{2,1,0:T(8,128)(2,1)S(1)} collective-permute-done((bf16[4,48,2048]{2,1,0:T(8,128)(2,1)S(1)}, bf16[4,48,2048]{2,1,0:T(8,128)(2,1)S(1)}, u32[]{:S(2)}, u32[]{:S(2)}) %collective-permute-start) | collective-permute-done | bytes 786464 | tf_op jit(solution)/shard_map/ppermute | solution.py:18
  31.5 0.0 copy-done
  31.5 0.0 copy-start.3
  31.5 0.8 %fusion = f32[192,768]{1,0:T(8,128)S(1)} fusion(bf16[192,2048]{1,0:T(8,128)(2,1)S(1)} %bitcast.39, bf16[1,1,2048,768]{3,2,1,0:T(8,128)(2,1)S(1)} %copy-done), kind=kOutput, calls=%fused_computation | convolution fusion | flops 603979776 | bytes 4521984 | tf_op jit(solution)/shard_map/dot_general | solution.py:23
  32.3 0.6 copy-done.3
  32.9 0.6 convolution_convert_fusion
  33.5 0.2 collective-permute-start.1
  33.7 0.8 %fusion.2 = f32[192,768]{1,0:T(8,128)S(1)} fusion(bf16[192,2048]{1,0:T(8,128)(2,1)S(1)} %bitcast.35, bf16[1,1,2048,768]{3,2,1,0:T(8,128)(2,1)S(1)} %copy-done), kind=kOutput, calls=%fused_computation.2 | convolution fusion | flops 603979776 | bytes 4521984 | tf_op jit(solution)/shard_map/dot_general | solution.py:23
  34.5 0.6 convolution_convert_fusion.1
  35.1 0.8 %collective-permute-done.1 = bf16[4,48,2048]{2,1,0:T(8,128)(2,1)S(1)} collective-permute-done((bf16[4,48,2048]{2,1,0:T(8,128)(2,1)S(1)}, bf16[4,48,2048]{2,1,0:T(8,128)(2,1)S(1)}, u32[]{:S(2)}, u32[]{:S(2)}) %collective-permute-start.1) | collective-permute-done | bytes 786464 | tf_op jit(solution)/shard_map/ppermute | solution.py:18
  35.8 0.0 copy-start.1
  35.8 0.0 copy-start.2
  35.8 0.3 fusion.5
  36.1 23.1 %all_to_all.11 = bf16[4,48,2048]{2,1,0:T(8,128)(2,1)S(1)} all-to-all(bf16[4,48,2048]{2,1,0:T(8,128)(2,1)S(1)} %fusion.5), channel_id=1, replica_groups=mesh['section'=4,'z'=4,'core'=2] {'z'}, dimensions={0} | all-to-all | bytes 1572864 | tf_op jit(solution)/shard_map/all_to_all | solution.py:99
  59.2 0.0 copy-done.1
  59.2 0.0 copy-done.2
  59.2 0.5 fusion.4
  59.7 1.5 %collective-permute-start.2 = (bf16[2,32,2048]{2,1,0:T(8,128)(2,1)S(1)}, bf16[2,32,2048]{2,1,0:T(8,128)(2,1)S(1)}, u32[]{:S(2)}, u32[]{:S(2)}) collective-permute-start(bf16[2,32,2048]{2,1,0:T(8,128)(2,1)S(1)} %fusion.4), channel_id=1, source_target_pairs={{0,8},{8,16},{16,24},{24,0},{1,9},{9,17},{17,25},{25,1},{2,10},{10... | collective-permute-start | bytes 786440 | tf_op jit(solution)/shard_map/ppermute | solution.py:14
  61.2 6.8 %collective-permute-done.2 = bf16[2,32,2048]{2,1,0:T(8,128)(2,1)S(1)} collective-permute-done((bf16[2,32,2048]{2,1,0:T(8,128)(2,1)S(1)}, bf16[2,32,2048]{2,1,0:T(8,128)(2,1)S(1)}, u32[]{:S(2)}, u32[]{:S(2)}) %collective-permute-start.2) | collective-permute-done | bytes 262176 | tf_op jit(solution)/shard_map/ppermute | solution.py:14
  68.0 0.7 %copy.10 = bf16[1,2,32,2048]{3,2,1,0:T(8,128)(2,1)} copy(bf16[1,2,32,2048]{3,2,1,0:T(8,128)(2,1)S(1)} %bitcast.40) | data formatting | bytes 524288
Async XLA Ops:
  0.0 31.5 %copy-start = (bf16[1,1,2048,768]{3,2,1,0:T(8,128)(2,1)S(1)}, bf16[1,1,2048,768]{3,2,1,0:T(8,128)(2,1)}, u32[]{:S(2)}) copy-start(bf16[1,1,2048,768]{3,2,1,0:T(8,128)(2,1)} %param.10) | copy-start | bytes 9437188
  29.2 2.3 %collective-permute-start = (bf16[4,48,2048]{2,1,0:T(8,128)(2,1)S(1)}, bf16[4,48,2048]{2,1,0:T(8,128)(2,1)S(1)}, u32[]{:S(2)}, u32[]{:S(2)}) collective-permute-start(bf16[4,48,2048]{2,1,0:T(8,128)(2,1)S(1)} %all_to_all.10), channel_id=1, source_target_pairs={{0,1},{1,0},{2,3},{3,2},{4,5},{5,4},{6,7},{7,6},{8,9},{9,8},{10,11... | collective-permute-start | bytes 2359304 | tf_op jit(solution)/shard_map/ppermute | solution.py:18
  31.5 1.4 %copy-start.3 = (bf16[1,1,384,2048]{3,2,1,0:T(8,128)(2,1)S(1)}, bf16[1,1,384,2048]{3,2,1,0:T(8,128)(2,1)}, u32[]{:S(2)}) copy-start(bf16[1,1,384,2048]{3,2,1,0:T(8,128)(2,1)} %param.11) | copy-start | bytes 4718596
  33.5 2.4 %collective-permute-start.1 = (bf16[4,48,2048]{2,1,0:T(8,128)(2,1)S(1)}, bf16[4,48,2048]{2,1,0:T(8,128)(2,1)S(1)}, u32[]{:S(2)}, u32[]{:S(2)}) collective-permute-start(bf16[4,48,2048]{2,1,0:T(8,128)(2,1)S(1)} %bitcast.43), channel_id=1, source_target_pairs={{0,1},{1,0},{2,3},{3,2},{4,5},{5,4},{6,7},{7,6},{8,9},{9,8},{10,11... | collective-permute-start | bytes 2359304 | tf_op jit(solution)/shard_map/ppermute | solution.py:18
  35.8 23.4 %copy-start.1 = (bf16[1,2,32,2048]{3,2,1,0:T(8,128)(2,1)S(1)}, bf16[1,2,32,2048]{3,2,1,0:T(8,128)(2,1)}, u32[]{:S(2)}) copy-start(bf16[1,2,32,2048]{3,2,1,0:T(8,128)(2,1)} %param.6) | copy-start | bytes 786436
  35.8 23.4 %copy-start.2 = (f32[2,192,32]{2,1,0:T(8,128)S(1)}, f32[2,192,32]{2,1,0:T(8,128)}, u32[]{:S(2)}) copy-start(f32[2,192,32]{2,1,0:T(8,128)} %get-tuple-element.7) | copy-start | bytes 147460
  59.7 8.3 %collective-permute-start.2 = (bf16[2,32,2048]{2,1,0:T(8,128)(2,1)S(1)}, bf16[2,32,2048]{2,1,0:T(8,128)(2,1)S(1)}, u32[]{:S(2)}, u32[]{:S(2)}) collective-permute-start(bf16[2,32,2048]{2,1,0:T(8,128)(2,1)S(1)} %fusion.4), channel_id=1, source_target_pairs={{0,8},{8,16},{16,24},{24,0},{1,9},{9,17},{17,25},{25,1},{2,10},{10... | collective-permute-start | bytes 786440 | tf_op jit(solution)/shard_map/ppermute | solution.py:14

commit v4 on v3

--- a/solution.py
+++ b/solution.py
@@ -40,13 +40,14 @@
     ).astype(jnp.float32)
     names = lax.broadcasted_iota(jnp.int32, (experts, tok_count), 0)
     lanes = lax.broadcasted_iota(jnp.int32, (slots, tok_count), 0)
+    columns = lax.broadcasted_iota(jnp.int32, (tok_count, slots), 1)
     buffer = jnp.zeros((slots, width), jnp.float32)
     for m in range(micro):
         routes = route_ref[m]
         weights = weight_ref[m]
         offset = jnp.zeros((experts, 1), jnp.float32)
         hit = jnp.zeros((slots, tok_count), jnp.float32)
-        mixing = jnp.zeros((slots, tok_count), jnp.float32)
+        mixing = jnp.zeros((tok_count, slots), jnp.float32)
         for k in range(topk):
             chosen = routes[k : k + 1, :]
             pick = (chosen == names).astype(jnp.float32)
@@ -55,7 +56,9 @@
             place = chosen * block + m * capacity + slot
             match = place == lanes
             hit = jnp.maximum(hit, match.astype(jnp.float32))
-            mixing = mixing + jnp.where(match, weights[k : k + 1, :], 0.0)
+            place_col = jnp.transpose(place)
+            weight_col = jnp.transpose(weights[k : k + 1, :])
+            mixing = mixing + jnp.where(place_col == columns, weight_col, 0.0)
             offset = offset + jnp.sum(pick, axis=1, keepdims=True)
         rows = normed[m * tok_count : (m + 1) * tok_count, :]
         buffer = buffer + jnp.dot(hit.astype(jnp.bfloat16), rows, preferred_element_type=jnp.float32)
@@ -70,7 +73,7 @@
         lambda *refs: prepare_kernel(*refs, experts=experts, capacity=capacity),
         out_shape=(
             jax.ShapeDtypeStruct((slots, width), jnp.bfloat16),
-            jax.ShapeDtypeStruct((micro, slots, tok_count), jnp.float32),
+            jax.ShapeDtypeStruct((micro, tok_count, slots), jnp.float32),
         ),
     )(
         inputs.reshape(micro * tok_count, width),
@@ -99,7 +102,7 @@
     returned = lax.all_to_all(results, "z", split_axis=0, concat_axis=0, tiled=True)
     table = returned.reshape(-1, width)
     combined = jnp.einsum(
-        "mqt,qd->mtd",
+        "mtq,qd->mtd",
         mixing,
         table.astype(jnp.float32),
         precision=lax.Precision.HIGH,

time: 68.9 us -> 68.9 us (level)
  no operation moved by 1% of the time
where the time goes in v4:
time: 68.9 us; the launch traced here: 68.7 us
  blocking collectives  49.6 us (72%)
  waiting for transfers between devices  9.84 us (14%)
  matrix products  3.14 us (5%)
  Pallas kernels  2.71 us (4%)
  starting transfers between devices  1.75 us (3%)
  local copies, waits for them, and re-layouts  1.34 us (2%)
    all_to_all x1, blocking collectives, body(): lax.all_to_all(buffer, 'z', split_axis=0, concat_axis=0, tiled=True)  26.5 us
    all_to_all x1, blocking collectives, body(): lax.all_to_all(results, 'z', split_axis=0, concat_axis=0, tiled=True)  23.1 us
    ppermute x1, waiting for transfers between devices, from_behind(): return lax.ppermute(value, axis, pairs)  6.79 us
    ppermute x2, waiting for transfers between devices, swap_cores(): return lax.ppermute(value, 'core', [(0, 1), (1, 0)])  3.04 us
    pallas_call x1, Pallas kernels, prepare(): pl.pallas_call(lambda *refs: prepare_kernel(*refs, experts=experts, capac...  2.71 us
    dot_general x2, matrix products, expert_half(): joined = jnp.dot(token_rows, weights_gu, preferred_element_type=jnp.float32)  1.55 us
    ppermute x1, starting transfers between devices, from_behind(): return lax.ppermute(value, axis, pairs)  1.54 us
  transfers between devices with their start and end apart: 3, of which 3 were waited for; matrix products, arithmetic and copies ran while one was open for 2% of the time, Pallas kernels for 0%

profile of v4, /device:TPU:0, one launch (start us, length us, event | category | flops | bytes accessed | tf_op | source)
XLA Modules:
  0.0 68.7 jit_solution(3916976522851153303)
XLA Ops:
  0.0 0.0 copy-start
  0.0 2.7 %shard_map.64 = (bf16[192,2048]{1,0:T(8,128)(2,1)}, f32[2,32,192]{2,1,0:T(8,128)}) custom-call(bf16[64,2048]{1,0:T(8,128)(2,1)} %bitcast.36, f32[1,2048]{1,0:T(1,128)} %refs_1_.1, s32[2,2,32]{2,1,0:T(2,128)} %bitcast.41, f32[2,2,32]{2,1,0:T(2,128)} %bitcast.42), custom_call_target="tpu_custom_call" | custom-call | tf_op jit(solution)/shard_map/pallas_call | solution.py:72
  2.7 26.5 %all_to_all.10 = bf16[4,48,2048]{2,1,0:T(8,128)(2,1)S(1)} all-to-all(bf16[4,48,2048]{2,1,0:T(8,128)(2,1)} %bitcast.37), channel_id=1, replica_groups=mesh['section'=4,'z'=4,'core'=2] {'z'}, dimensions={0} | all-to-all | bytes 1572864 | tf_op jit(solution)/shard_map/all_to_all | solution.py:95
  29.2 0.0 collective-permute-start
  29.2 2.3 %collective-permute-done = bf16[4,48,2048]{2,1,0:T(8,128)(2,1)S(1)} collective-permute-done((bf16[4,48,2048]{2,1,0:T(8,128)(2,1)S(1)}, bf16[4,48,2048]{2,1,0:T(8,128)(2,1)S(1)}, u32[]{:S(2)}, u32[]{:S(2)}) %collective-permute-start) | collective-permute-done | bytes 786464 | tf_op jit(solution)/shard_map/ppermute | solution.py:18
  31.5 0.0 copy-done
  31.5 0.0 copy-start.3
  31.5 0.8 %fusion = f32[192,768]{1,0:T(8,128)S(1)} fusion(bf16[192,2048]{1,0:T(8,128)(2,1)S(1)} %bitcast.39, bf16[1,1,2048,768]{3,2,1,0:T(8,128)(2,1)S(1)} %copy-done), kind=kOutput, calls=%fused_computation | convolution fusion | flops 603979776 | bytes 4521984 | tf_op jit(solution)/shard_map/dot_general | solution.py:23
  32.2 0.6 copy-done.3
  32.9 0.6 convolution_convert_fusion
  33.5 0.2 collective-permute-start.1
  33.7 0.8 %fusion.2 = f32[192,768]{1,0:T(8,128)S(1)} fusion(bf16[192,2048]{1,0:T(8,128)(2,1)S(1)} %bitcast.35, bf16[1,1,2048,768]{3,2,1,0:T(8,128)(2,1)S(1)} %copy-done), kind=kOutput, calls=%fused_computation.2 | convolution fusion | flops 603979776 | bytes 4521984 | tf_op jit(solution)/shard_map/dot_general | solution.py:23
  34.5 0.6 convolution_convert_fusion.1
  35.1 0.8 %collective-permute-done.1 = bf16[4,48,2048]{2,1,0:T(8,128)(2,1)S(1)} collective-permute-done((bf16[4,48,2048]{2,1,0:T(8,128)(2,1)S(1)}, bf16[4,48,2048]{2,1,0:T(8,128)(2,1)S(1)}, u32[]{:S(2)}, u32[]{:S(2)}) %collective-permute-start.1) | collective-permute-done | bytes 786464 | tf_op jit(solution)/shard_map/ppermute | solution.py:18
  35.8 0.0 copy-start.1
  35.8 0.0 copy-start.2
  35.8 0.3 fusion.5
  36.1 23.1 %all_to_all.11 = bf16[4,48,2048]{2,1,0:T(8,128)(2,1)S(1)} all-to-all(bf16[4,48,2048]{2,1,0:T(8,128)(2,1)S(1)} %fusion.5), channel_id=1, replica_groups=mesh['section'=4,'z'=4,'core'=2] {'z'}, dimensions={0} | all-to-all | bytes 1572864 | tf_op jit(solution)/shard_map/all_to_all | solution.py:102
  59.2 0.0 copy-done.1
  59.2 0.0 copy-done.2
  59.2 0.4 fusion.4
  59.6 1.5 %collective-permute-start.2 = (bf16[2,32,2048]{2,1,0:T(8,128)(2,1)S(1)}, bf16[2,32,2048]{2,1,0:T(8,128)(2,1)S(1)}, u32[]{:S(2)}, u32[]{:S(2)}) collective-permute-start(bf16[2,32,2048]{2,1,0:T(8,128)(2,1)S(1)} %fusion.4), channel_id=1, source_target_pairs={{0,8},{8,16},{16,24},{24,0},{1,9},{9,17},{17,25},{25,1},{2,10},{10... | collective-permute-start | bytes 786440 | tf_op jit(solution)/shard_map/ppermute | solution.py:14
  61.2 6.8 %collective-permute-done.2 = bf16[2,32,2048]{2,1,0:T(8,128)(2,1)S(1)} collective-permute-done((bf16[2,32,2048]{2,1,0:T(8,128)(2,1)S(1)}, bf16[2,32,2048]{2,1,0:T(8,128)(2,1)S(1)}, u32[]{:S(2)}, u32[]{:S(2)}) %collective-permute-start.2) | collective-permute-done | bytes 262176 | tf_op jit(solution)/shard_map/ppermute | solution.py:14
  67.9 0.7 %copy.8 = bf16[1,2,32,2048]{3,2,1,0:T(8,128)(2,1)} copy(bf16[1,2,32,2048]{3,2,1,0:T(8,128)(2,1)S(1)} %bitcast.40) | data formatting | bytes 524288
Async XLA Ops:
  0.0 31.5 %copy-start = (bf16[1,1,2048,768]{3,2,1,0:T(8,128)(2,1)S(1)}, bf16[1,1,2048,768]{3,2,1,0:T(8,128)(2,1)}, u32[]{:S(2)}) copy-start(bf16[1,1,2048,768]{3,2,1,0:T(8,128)(2,1)} %param.10) | copy-start | bytes 9437188
  29.2 2.3 %collective-permute-start = (bf16[4,48,2048]{2,1,0:T(8,128)(2,1)S(1)}, bf16[4,48,2048]{2,1,0:T(8,128)(2,1)S(1)}, u32[]{:S(2)}, u32[]{:S(2)}) collective-permute-start(bf16[4,48,2048]{2,1,0:T(8,128)(2,1)S(1)} %all_to_all.10), channel_id=1, source_target_pairs={{0,1},{1,0},{2,3},{3,2},{4,5},{5,4},{6,7},{7,6},{8,9},{9,8},{10,11... | collective-permute-start | bytes 2359304 | tf_op jit(solution)/shard_map/ppermute | solution.py:18
  31.5 1.4 %copy-start.3 = (bf16[1,1,384,2048]{3,2,1,0:T(8,128)(2,1)S(1)}, bf16[1,1,384,2048]{3,2,1,0:T(8,128)(2,1)}, u32[]{:S(2)}) copy-start(bf16[1,1,384,2048]{3,2,1,0:T(8,128)(2,1)} %param.11) | copy-start | bytes 4718596
  33.5 2.4 %collective-permute-start.1 = (bf16[4,48,2048]{2,1,0:T(8,128)(2,1)S(1)}, bf16[4,48,2048]{2,1,0:T(8,128)(2,1)S(1)}, u32[]{:S(2)}, u32[]{:S(2)}) collective-permute-start(bf16[4,48,2048]{2,1,0:T(8,128)(2,1)S(1)} %bitcast.43), channel_id=1, source_target_pairs={{0,1},{1,0},{2,3},{3,2},{4,5},{5,4},{6,7},{7,6},{8,9},{9,8},{10,11... | collective-permute-start | bytes 2359304 | tf_op jit(solution)/shard_map/ppermute | solution.py:18
  35.8 23.4 %copy-start.1 = (bf16[1,2,32,2048]{3,2,1,0:T(8,128)(2,1)S(1)}, bf16[1,2,32,2048]{3,2,1,0:T(8,128)(2,1)}, u32[]{:S(2)}) copy-start(bf16[1,2,32,2048]{3,2,1,0:T(8,128)(2,1)} %param.6) | copy-start | bytes 786436
  35.8 23.4 %copy-start.2 = (f32[2,32,192]{2,1,0:T(8,128)S(1)}, f32[2,32,192]{2,1,0:T(8,128)}, u32[]{:S(2)}) copy-start(f32[2,32,192]{2,1,0:T(8,128)} %get-tuple-element.7) | copy-start | bytes 147460
  59.6 8.3 %collective-permute-start.2 = (bf16[2,32,2048]{2,1,0:T(8,128)(2,1)S(1)}, bf16[2,32,2048]{2,1,0:T(8,128)(2,1)S(1)}, u32[]{:S(2)}, u32[]{:S(2)}) collective-permute-start(bf16[2,32,2048]{2,1,0:T(8,128)(2,1)S(1)} %fusion.4), channel_id=1, source_target_pairs={{0,8},{8,16},{16,24},{24,0},{1,9},{9,17},{17,25},{25,1},{2,10},{10... | collective-permute-start | bytes 786440 | tf_op jit(solution)/shard_map/ppermute | solution.py:14
